TPU v7x, 128 devices: a whole 4x4x4 slice. The times are simulated.
128 devices in a mesh: panel: 16 (over z_hi, y, core), col: 8 (over z_lo, x).
Axes of the slice: x: 4, y: 4, z: 4 (z_hi: 2, z_lo: 2; z = z_hi * 2 + z_lo), core: 2. Of those that a mesh axis runs over, the one named last changes fastest.
Arguments:
- panel_rows: bfloat16 [32768, 512], P(('panel', 'col')), may hold values from -6 to 6
- diag_blocks: float32 [512, 512], replicated
- adjoint: bfloat16 [32768, 32768], P('panel', 'col')
- fill: int32 [128, 128], P('panel', 'col'), may hold values from 0 to 1, as said below
Outputs:
- grad_panel: float32 [32768, 512], P(('panel', 'col'))
- grad_diag: float32 [512, 512], replicated
Inputs may be any that keep to these rules, and one draw needn't show every extreme that they name: fill is 1 on every diagonal block, fill equals its transpose, and adjoint equals its transpose.
All inputs are finite; a program needn't handle non-finite values.
Results may differ from a plain program's by a relative error of at most 0.004.
Values may be sent and summed in bfloat16 or wider, within the bound.
No kernel may reach another device: no remote copies, remote signals or barrier semaphores. Data moves between devices by JAX's collectives and lax.ppermute only.
A program may use at most 128 MiB of HBM per device.

v0:
```python
import jax
import jax.numpy as jnp
from jax import lax
from jax.sharding import PartitionSpec as P

B = 256


def broadcast(shard, axis, root):
    mine = lax.axis_index(axis) == root
    return lax.psum(jnp.where(mine, shard, jnp.zeros_like(shard)), axis)


def factor_with_logdet(matrix):
    lower = jnp.linalg.cholesky(matrix)
    return (lower, 2.0 * jnp.sum(jnp.log(jnp.diagonal(lower))))


def shards(panel_rows, diag_blocks, adjoint, fill):
    lower = jnp.linalg.cholesky(diag_blocks)
    scaled = jax.scipy.linalg.solve_triangular(
        lower, panel_rows.astype(jnp.float32).T, lower=True
    ).T.astype(jnp.bfloat16)
    piece = scaled.shape[0]
    n_col = lax.axis_size("col")
    n_pan = lax.axis_size("panel")
    groups = n_pan // n_col
    panel_block = lax.all_gather(scaled, "col", axis=0, tiled=True)
    parts = []
    for offset in range(groups):
        root = lax.axis_index("col") * groups + offset
        parts.append(broadcast(panel_block, "panel", root))
    columns = jnp.concatenate(parts, 0)
    row_fill = jnp.repeat(fill, B, axis=0)
    col_blocks = fill.shape[1]
    marks = row_fill.astype(jnp.bfloat16)
    masked = (
        adjoint.reshape(lax.axis_size("col") * piece, col_blocks, B) * marks[:, :, None]
    ).reshape(lax.axis_size("col") * piece, col_blocks * B)
    summed = lax.psum_scatter(
        jnp.dot(masked, columns, preferred_element_type=jnp.float32),
        "col",
        scatter_dimension=0,
        tiled=True,
    )
    grad_scaled = -summed
    grad_panel = jax.scipy.linalg.solve_triangular(lower, grad_scaled.T, lower=True, trans=1).T
    partial_lower = -jnp.dot(
        grad_panel.T, scaled.astype(jnp.float32), precision=lax.Precision.HIGHEST
    )
    grad_lower = jnp.tril(lax.psum(partial_lower, ("panel", "col")))
    outputs, pullback = jax.vjp(factor_with_logdet, diag_blocks)
    grad_diag = pullback((grad_lower, jnp.ones((), jnp.float32)))[0]
    return (grad_panel, grad_diag)


def solution(mesh):
    in_specs = (P(("panel", "col"), None), P(), P("panel", "col"), P("panel", "col"))
    out_specs = (P(("panel", "col"), None), P())
    return jax.shard_map(shards, mesh=mesh, in_specs=in_specs, out_specs=out_specs, check_vma=False)
```

profile of v0, /device:TPU:1, one launch (start us, length us, event | category | flops | bytes accessed | tf_op | source)
XLA Modules:
  0.0 620.1 jit_solution(10813979007335446969)
XLA Ops:
  7.2 1.6 copy.11
  8.8 1.4 fusion.8
  10.3 11.7 %custom-call.42 = f32[128,128]{1,0:T(8,128)S(1)} custom-call(f32[128,128]{1,0:T(8,128)S(1)} %slice.221), custom_call_target="Cholesky" | custom-call | tf_op jit(solution)/shard_map/jit(cholesky)/cholesky/custom-call.4 | solution.py:20
  22.0 9.8 %custom-call.43 = f32[1,128,128]{1,2,0:T(8,128)S(1)} custom-call(f32[1,128,128]{2,1,0:T(8,128)S(1)} %get-tuple-element.44), custom_call_target="InvertDiagBlocksLowerTriangular" | custom-call | tf_op jit(solution)/shard_map/jit(cholesky)/cholesky/custom-call.11 | solution.py:20
  32.9 11.7 %custom-call.44 = f32[128,128]{1,0:T(8,128)S(1)} custom-call(f32[128,128]{1,0:T(8,128)S(1)} %slice.225), custom_call_target="Cholesky" | custom-call | tf_op jit(solution)/shard_map/jit(cholesky)/cholesky/custom-call.5 | solution.py:20
  44.8 10.0 %custom-call.45 = f32[1,128,128]{1,2,0:T(8,128)S(1)} custom-call(f32[1,128,128]{2,1,0:T(8,128)S(1)} %get-tuple-element.41), custom_call_target="InvertDiagBlocksLowerTriangular" | custom-call | tf_op jit(solution)/shard_map/jit(cholesky)/cholesky/custom-call.12 | solution.py:20
  55.4 11.7 %custom-call.46 = f32[128,128]{1,0:T(8,128)S(1)} custom-call(f32[128,128]{1,0:T(8,128)S(1)} %slice.230), custom_call_target="Cholesky" | custom-call | tf_op jit(solution)/shard_map/jit(cholesky)/cholesky/custom-call.6 | solution.py:20
  67.2 9.8 %custom-call.47 = f32[1,128,128]{1,2,0:T(8,128)S(1)} custom-call(f32[1,128,128]{2,1,0:T(8,128)S(1)} %get-tuple-element.38), custom_call_target="InvertDiagBlocksLowerTriangular" | custom-call | tf_op jit(solution)/shard_map/jit(cholesky)/cholesky/custom-call.13 | solution.py:20
  77.6 12.1 %custom-call.48 = f32[128,128]{1,0:T(8,128)S(1)} custom-call(f32[128,128]{1,0:T(8,128)S(1)} %convolution_subtract_fusion.14), custom_call_target="Cholesky" | custom-call | tf_op jit(solution)/shard_map/jit(cholesky)/cholesky/custom-call.7 | solution.py:20
  94.4 8.5 %while.1 = (s32[]{:T(128)}, f32[512,512]{1,0:T(8,128)S(1)}, s32[4,2]{0,1:T(2,128)S(1)}, f32[4,128,128]{2,1,0:T(8,128)S(1)}, s32[]{:T(128)}) while((s32[]{:T(128)}, f32[512,512]{1,0:T(8,128)S(1)}, s32[4,2]{0,1:T(2,128)S(1)}, f32[4,128,128]{2,1,0:T(8,128)S(1)}, s32[]{:T(128)}) %tuple.45), condition=%wide.while_cond, body=%wide.while_body.sunk | while | flops 2 | bytes 131189 | solution.py:47
  95.1 1.4 bitcast_dynamic-update-slice_fusion.2
  97.2 1.4 bitcast_dynamic-update-slice_fusion.2
  99.4 1.4 bitcast_dynamic-update-slice_fusion.2
  101.5 1.4 bitcast_dynamic-update-slice_fusion.2
  102.9 39.3 %custom-call.37 = f32[4,128,128]{1,2,0:T(8,128)S(1)} custom-call(f32[4,128,128]{2,1,0:T(8,128)S(1)} %get-tuple-element.16), custom_call_target="InvertDiagBlocksLowerTriangular" | custom-call | tf_op jit(solution)/shard_map/jit(_solve_triangular)/triangular_solve | solution.py:47
  146.2 44.2 %all-gather.2.cloned.1.call-done = bf16[2048,512]{0,1:T(8,128)(2,1)} async-done(((bf16[256,512]{0,1:T(8,128)(2,1)}), bf16[2048,512]{0,1:T(8,128)(2,1)}) %all-gather.2.cloned.1.call-update) | async-done | bytes 2097168 | tf_op jit(solution)/shard_map/all_gather | solution.py:28
  190.4 3.8 broadcast_select_fusion.1
  194.3 4.9 mul.15
  199.3 10.7 %copy.16 = bf16[256,8,16,256]{3,1,2,0:T(8,128)(2,1)} copy(bf16[256,8,16,256]{3,2,1,0:T(8,128)(2,1)S(1)} %bitcast.99) | data formatting | bytes 33554432
  210.0 140.1 %all-reduce.7.cloned.1.call-done = (bf16[2048,512]{0,1:T(8,128)(2,1)}, bf16[2048,512]{0,1:T(8,128)(2,1)}) async-done(((bf16[2048,512]{0,1:T(8,128)(2,1)}, bf16[2048,512]{0,1:T(8,128)(2,1)}), (bf16[2048,512]{0,1:T(8,128)(2,1)}, bf16[2048,512]{0,1:T(8,128)(2,1)})) %all-reduce.7.cloned.1.call-update) | async-done | bytes 4194320 | tf_op jit(solution)/shard_map/psum | solution.py:11
  350.0 17.6 %fusion = f32[2048,512]{1,0:T(8,128)} fusion(bf16[2048,4096]{1,0:T(8,128)(2,1)} %param.7, bf16[2048,4096]{1,0:T(8,128)(2,1)} %bitcast.102, bf16[2048,512]{0,1:T(8,128)(2,1)} %get-tuple-element.29, bf16[2048,512]{0,1:T(8,128)(2,1)} %get-tuple-element.30), kind=kOutput, calls=%fused_computation.4 | convolution fusion | flops 8606711808 | bytes 41943040 | tf_op jit(solution)/shard_map/dot_general | solution.py:41
  367.8 4.5 gather_fusion
  372.4 49.8 %reduce-scatter.2.cloned.1.call-done = f32[256,512]{1,0:T(8,128)} async-done(((f32[2048,512]{1,0:T(8,128)}), f32[256,512]{1,0:T(8,128)}) %reduce-scatter.2.cloned.1.call-update) | async-done | bytes 524304 | tf_op jit(solution)/shard_map/reduce_scatter | solution.py:40
  422.2 1.1 negate_bitcast_fusion
  426.2 1.6 convolution_negate_fusion
  428.9 145.2 %all-reduce.5.cloned.1.call-done = f32[512,512]{1,0:T(8,128)} async-done(((f32[512,512]{1,0:T(8,128)}), f32[512,512]{1,0:T(8,128)}) %all-reduce.5.cloned.1.call-update) | async-done | bytes 1048592 | tf_op jit(solution)/shard_map/psum | solution.py:51
  574.1 1.4 fusion.11
  575.5 26.0 %scatter_fusion = f32[512,512]{1,0:T(8,128)S(1)} fusion(f32[512,512]{1,0:T(8,128)S(1)} %fusion.11, s32[512]{0:T(512)S(1)} %bitcast.100, f32[512]{0:T(512)S(1)} %broadcast_divide_fusion), kind=kCustom, calls=%fused_computation.1 | custom fusion | flops 512 | bytes 10240 | tf_op jit(solution)/shard_map/transpose(jvp(jit(diagonal)))/cond/branch_0_fun/scatter-add | solution.py:16
  601.5 1.9 fusion.5
  608.0 1.0 convolution_subtract_fusion
  609.4 1.5 convolution_subtract_fusion.4
  612.2 1.2 bitcast_add_fusion
  (84 shorter events, 21.8 us)
Async XLA Ops:
  7.2 183.2 %all-gather.2.cloned.1.call-start = ((), (), s32[]{:S(2)}) async-start(), calls=%async_computation.1 | async-start | bytes 2359296 | tf_op jit(solution)/shard_map/all_gather | solution.py:28
  22.0 120.3 %copy-start = (bf16[256,512]{1,0:T(8,128)(2,1)S(1)}, bf16[256,512]{1,0:T(8,128)(2,1)}, u32[]{:S(2)}) copy-start(bf16[256,512]{1,0:T(8,128)(2,1)} %param.5) | copy-start | bytes 786436
  146.1 203.9 %all-reduce.7.cloned.1.call-start = ((), (), s32[]{:S(2)}) async-start(), calls=%async_computation.4 | async-start | bytes 8388608 | tf_op jit(solution)/shard_map/psum | solution.py:11
  146.2 48.1 %copy-start.1 = (s32[8,16]{1,0:T(8,128)S(1)}, s32[8,16]{1,0:T(8,128)}, u32[]{:S(2)}) copy-start(s32[8,16]{1,0:T(8,128)} %param.8) | copy-start | bytes 1540
  194.2 228.0 %reduce-scatter.2.cloned.1.call-start = ((), (), s32[]{:S(2)}) async-start(), calls=%async_computation.2 | async-start | bytes 4718592 | tf_op jit(solution)/shard_map/reduce_scatter | solution.py:40
  367.6 206.5 %all-reduce.5.cloned.1.call-start = ((), (), s32[]{:S(2)}) async-start(), calls=%async_computation.3 | async-start | bytes 2097152 | tf_op jit(solution)/shard_map/psum | solution.py:51
Sparse Core Ops, SparseCore 0:
  146.2 44.0 all-gather.1
  194.3 155.6 all-reduce.6
  367.7 54.4 reduce-scatter.1
  428.0 146.1 all-reduce.4
where the time goes:
time: 629 us; the launch traced here: 620 us
  waiting for transfers between devices  379 us (60%)
  other arithmetic  155 us (25%)
  matrix products  36.6 us (6%)
  local copies, waits for them, and re-layouts  32.1 us (5%)
  between operations  17.1 us (3%)
    psum x1, waiting for transfers between devices, shards(): grad_lower = jnp.tril(lax.psum(partial_lower, ('panel', 'col')))  145 us
    psum x1, waiting for transfers between devices, broadcast(): return lax.psum(jnp.where(mine, shard, jnp.zeros_like(shard)), axis)  140 us
    another operation x14, other arithmetic, shards(): lower = jnp.linalg.cholesky(diag_blocks)  79 us
    reduce_scatter x1, waiting for transfers between devices, shards(): lax.psum_scatter(jnp.dot(masked, columns, preferred_element_type=jnp.floa...  49.8 us
    all_gather x1, waiting for transfers between devices, shards(): panel_block = lax.all_gather(scaled, 'col', axis=0, tiled=True)  44.2 us
    another operation x3, other arithmetic, shards(): jax.scipy.linalg.solve_triangular(lower, grad_scaled.T, lower=True, trans=1)  39.4 us
    scatter-add x1, other arithmetic, factor_with_logdet(): return (lower, 2.0 * jnp.sum(jnp.log(jnp.diagonal(lower))))  26 us
    dot_general x1, matrix products, shards(): jnp.dot(masked, columns, preferred_element_type=jnp.float32)  17.6 us
  transfers between devices with their start and end apart: 4, of which 4 were waited for; matrix products, arithmetic and copies ran while one was open for 3% of the time, Pallas kernels for 0%

commit v1 on v0

v1 whole, which is shorter than its diff:
```python
import jax
import jax.numpy as jnp
from jax import lax
from jax.sharding import PartitionSpec as P

B = 256
F32 = jnp.float32
BF16 = jnp.bfloat16
HIGHEST = lax.Precision.HIGHEST


def shift(x, axis, n, s):
    return lax.ppermute(x, axis, [(i, (i + s) % n) for i in range(n)])


def gather_ring(x, axis, n, me):
    got = [x] + [shift(x, axis, n, s) for s in range(1, n)]
    held = jnp.stack([got[(-m) % n] for m in range(n)])
    return jnp.roll(held, me, axis=0).reshape((-1,) + x.shape[1:])


def scatter_sum(x, axis, n, me):
    rows = x.shape[0] // n
    acc = lax.dynamic_slice_in_dim(x, me * rows, rows, 0)
    for s in range(1, n):
        part = lax.dynamic_slice_in_dim(x, ((me + s) % n) * rows, rows, 0)
        acc = acc + shift(part, axis, n, s)
    return acc


def all_sum(x, n_col, n_pan, c, p):
    y = scatter_sum(x, "col", n_col, c)
    z = scatter_sum(y, "panel", n_pan, p)
    y = gather_ring(z, "panel", n_pan, p)
    return gather_ring(y, "col", n_col, c)


def split3(w):
    hi = lax.reduce_precision(w, exponent_bits=8, mantissa_bits=7)
    r = w - hi
    mid = lax.reduce_precision(r, exponent_bits=8, mantissa_bits=7)
    lo = r - mid
    return hi.astype(BF16), mid.astype(BF16), lo.astype(BF16)


def apply_split(x, parts):
    hi, mid, lo = parts
    d = lambda w: jnp.dot(x, w, preferred_element_type=F32)
    return d(hi) + (d(mid) + d(lo))


def shards(panel_rows, diag_blocks, adjoint, fill):
    n_col = lax.axis_size("col")
    n_pan = lax.axis_size("panel")
    c = lax.axis_index("col")
    p = lax.axis_index("panel")
    piece, width = panel_rows.shape

    flat = n_pan * n_col
    perm = [((dst % n_col) * n_pan + dst // n_col, dst) for dst in range(flat)]
    mine = lax.ppermute(panel_rows, ("panel", "col"), perm)
    col_rows = lax.all_gather(mine, "panel", axis=0, tiled=True)

    lower = jnp.linalg.cholesky(diag_blocks)
    linv = jax.scipy.linalg.solve_triangular(lower, jnp.eye(width, dtype=F32), lower=True)
    parts = split3(linv.T)
    scaled_cols = apply_split(col_rows, parts).astype(BF16)
    scaled = apply_split(panel_rows, parts).astype(BF16)

    marks = fill.astype(BF16)
    col_blocks = fill.shape[1]
    per = piece // B

    def product(k):
        rows = lax.dynamic_slice_in_dim(adjoint, k * piece, piece, 0)
        m = lax.dynamic_slice_in_dim(marks, k * per, per, 0)
        masked = (rows.reshape(per, B, col_blocks, B) * m[:, None, :, None]).reshape(piece, -1)
        return jnp.dot(masked, scaled_cols, preferred_element_type=F32)

    total = product(c)
    for s in range(1, n_col):
        total = total + shift(product((c + s) % n_col), "col", n_col, s)
    grad_scaled = -total
    grad_panel = jnp.dot(grad_scaled, linv, precision=HIGHEST)
    partial_lower = -jnp.dot(grad_panel.T, scaled.astype(F32), precision=HIGHEST)
    grad_lower = jnp.tril(all_sum(partial_lower, n_col, n_pan, c, p))

    diag = jnp.diagonal(lower)
    eye = jnp.eye(width, dtype=F32)
    bar = grad_lower + eye * (2.0 / diag)[None, :]
    inner = jnp.tril(jnp.dot(lower.T, bar, precision=HIGHEST)) * (1.0 - 0.5 * eye)
    sigma = jnp.dot(jnp.dot(linv.T, inner, precision=HIGHEST), linv, precision=HIGHEST)
    grad_diag = 0.5 * (sigma + sigma.T)
    return (grad_panel, grad_diag)


def solution(mesh):
    in_specs = (P(("panel", "col"), None), P(), P("panel", "col"), P("panel", "col"))
    out_specs = (P(("panel", "col"), None), P())
    return jax.shard_map(shards, mesh=mesh, in_specs=in_specs, out_specs=out_specs, check_vma=False)
```

time: 629 us -> 406 us (0.65)
  waiting for transfers between devices: 379 us -> 62.5 us
  starting transfers between devices: 0.33 us -> 95.6 us
  matrix products: 36.6 us -> 68.4 us
  other arithmetic: 155 us -> 134 us
  local copies, waits for them, and re-layouts: 32.1 us -> 20.6 us
    psum x2 -> x0, waiting for transfers between devices: 285 us -> none  [the longest x1 145 us: shards(): grad_lower = jnp.tril(lax.psum(partial_lower, ('panel', 'col')))]
    ppermute x0 -> x52, starting transfers between devices: none -> 95.6 us  [the longest x51 88.7 us: shift(): return lax.ppermute(x, axis, [(i, (i + s) % n) for i in range(n)])]
    ppermute x0 -> x52, waiting for transfers between devices: none -> 62.5 us  [the longest x51 56.1 us: shift(): return lax.ppermute(x, axis, [(i, (i + s) % n) for i in range(n)])]
    reduce_scatter x1 -> x0, waiting for transfers between devices: 49.8 us -> none  [shards(): lax.psum_scatter(jnp.dot(masked, columns, preferred_element_type=jnp.floa...]
    all_gather x1, waiting for transfers between devices: 44.2 us -> 0.02 us  [shards(): col_rows = lax.all_gather(mine, 'panel', axis=0, tiled=True)]
    dot_general x3 -> x19, matrix products: 21 us -> 63.5 us  [the longest x8 30.7 us: product(): return jnp.dot(masked, scaled_cols, preferred_element_type=F32)]
    scatter-add x1 -> x0, other arithmetic: 26 us -> none  [factor_with_logdet(): return (lower, 2.0 * jnp.sum(jnp.log(jnp.diagonal(lower))))]
    another operation x28 -> x7, matrix products: 13.5 us -> 3.01 us  [shards(): jax.scipy.linalg.solve_triangular(lower, jnp.eye(width, dtype=F32), lower...]
  transfers between devices with their start and end apart: 4 -> 53, of which waited for: 4 -> 17; matrix products, arithmetic and copies ran while one was open for 3% -> 45% of each run, Pallas kernels for 0% -> 0%
where the time goes in v1:
time: 406 us; the launch traced here: 398 us
  other arithmetic  134 us (33%)
  starting transfers between devices  95.6 us (24%)
  matrix products  68.4 us (17%)
  waiting for transfers between devices  62.5 us (15%)
  local copies, waits for them, and re-layouts  20.6 us (5%)
  between operations  17.8 us (4%)
    another operation x14, other arithmetic, shards(): lower = jnp.linalg.cholesky(diag_blocks)  88.9 us
    ppermute x51, starting transfers between devices, shift(): return lax.ppermute(x, axis, [(i, (i + s) % n) for i in range(n)])  88.7 us
    ppermute x51, waiting for transfers between devices, shift(): return lax.ppermute(x, axis, [(i, (i + s) % n) for i in range(n)])  56.1 us
    another operation x3, other arithmetic, shards(): jax.scipy.linalg.solve_triangular(lower, jnp.eye(width, dtype=F32), lower...  40.4 us
    dot_general x8, matrix products, product(): return jnp.dot(masked, scaled_cols, preferred_element_type=F32)  30.7 us
    dot_general x6, matrix products, apply_split(): d = lambda w: jnp.dot(x, w, preferred_element_type=F32)  25.1 us
    another operation x12, local copies, waits for them, and re-layouts  10.5 us
  transfers between devices with their start and end apart: 53, of which 17 were waited for; matrix products, arithmetic and copies ran while one was open for 45% of the time, Pallas kernels for 0%

profile of v1, /device:TPU:1, one launch (start us, length us, event | category | flops | bytes accessed | tf_op | source)
XLA Modules:
  0.0 398.4 jit_solution(12658101298553064213)
XLA Ops:
  7.2 6.9 %collective-permute-start = (bf16[256,512]{1,0:T(8,128)(2,1)}, bf16[256,512]{1,0:T(8,128)(2,1)S(1)}, u32[]{:S(2)}, u32[]{:S(2)}) collective-permute-start(bf16[256,512]{1,0:T(8,128)(2,1)} %param.4), channel_id=1, source_target_pairs={{0,0},{16,1},{32,2},{48,3},{64,4},{80,5},{96,6},{112,7},{1,8},{17,... | collective-permute-start | bytes 786440 | tf_op jit(solution)/shard_map/ppermute | solution.py:61
  14.1 6.4 %collective-permute-done = bf16[256,512]{1,0:T(8,128)(2,1)S(1)} collective-permute-done((bf16[256,512]{1,0:T(8,128)(2,1)}, bf16[256,512]{1,0:T(8,128)(2,1)S(1)}, u32[]{:S(2)}, u32[]{:S(2)}) %collective-permute-start) | collective-permute-done | bytes 262176 | tf_op jit(solution)/shard_map/ppermute | solution.py:61
  24.4 11.7 %cholesky.104 = f32[128,128]{1,0:T(8,128)S(1)} custom-call(f32[128,128]{1,0:T(8,128)S(1)} %cholesky.266), custom_call_target="Cholesky" | custom-call | tf_op jit(solution)/shard_map/jit(cholesky)/cholesky | solution.py:64
  36.3 9.8 %custom-call.31 = f32[1,128,128]{1,2,0:T(8,128)S(1)} custom-call(f32[1,128,128]{2,1,0:T(8,128)S(1)} %get-tuple-element.55), custom_call_target="InvertDiagBlocksLowerTriangular" | custom-call | tf_op jit(solution)/shard_map/jit(cholesky)/cholesky | solution.py:64
  46.8 11.7 %cholesky.217 = f32[128,128]{1,0:T(8,128)S(1)} custom-call(f32[128,128]{1,0:T(8,128)S(1)} %cholesky.270), custom_call_target="Cholesky" | custom-call | tf_op jit(solution)/shard_map/jit(cholesky)/cholesky | solution.py:64
  58.5 10.0 %custom-call.32 = f32[1,128,128]{1,2,0:T(8,128)S(1)} custom-call(f32[1,128,128]{2,1,0:T(8,128)S(1)} %get-tuple-element.52), custom_call_target="InvertDiagBlocksLowerTriangular" | custom-call | tf_op jit(solution)/shard_map/jit(cholesky)/cholesky | solution.py:64
  69.3 11.7 %cholesky.238 = f32[128,128]{1,0:T(8,128)S(1)} custom-call(f32[128,128]{1,0:T(8,128)S(1)} %cholesky.275), custom_call_target="Cholesky" | custom-call | tf_op jit(solution)/shard_map/jit(cholesky)/cholesky | solution.py:64
  81.0 9.8 %custom-call.33 = f32[1,128,128]{1,2,0:T(8,128)S(1)} custom-call(f32[1,128,128]{2,1,0:T(8,128)S(1)} %get-tuple-element.49), custom_call_target="InvertDiagBlocksLowerTriangular" | custom-call | tf_op jit(solution)/shard_map/jit(cholesky)/cholesky | solution.py:64
  91.4 11.7 %cholesky.255 = f32[128,128]{1,0:T(8,128)S(1)} custom-call(f32[128,128]{1,0:T(8,128)S(1)} %convolution_subtract_fusion.5), custom_call_target="Cholesky" | custom-call | tf_op jit(solution)/shard_map/jit(cholesky)/cholesky | solution.py:64
  106.5 10.8 %compare_reduce_fusion = pred[]{:T(512)} fusion(f32[128]{0:T(128)S(1)} %get-tuple-element.46), kind=kLoop, calls=%fused_computation.232 | loop fusion | flops 255 | bytes 513 | tf_op jit(solution)/shard_map/jit(cholesky)/cholesky | solution.py:64
  118.2 10.6 %while.1 = (s32[]{:T(128)}, f32[512,512]{1,0:T(8,128)S(1)}, s32[4,2]{0,1:T(2,128)S(1)}, f32[4,128,128]{2,1,0:T(8,128)}, s32[]{:T(128)}) while((s32[]{:T(128)}, f32[512,512]{1,0:T(8,128)S(1)}, s32[4,2]{0,1:T(2,128)S(1)}, f32[4,128,128]{2,1,0:T(8,128)}, s32[]{:T(128)}) %tuple.64), condition=%wide.while_cond, body=%wide.while_body.sunk | while | flops 2 | bytes 132205 | solution.py:65
  128.7 40.1 %custom-call.34 = f32[4,128,128]{1,2,0:T(8,128)S(1)} custom-call(f32[4,128,128]{2,1,0:T(8,128)} %get-tuple-element.9), custom_call_target="InvertDiagBlocksLowerTriangular" | custom-call | tf_op jit(solution)/shard_map/jit(_solve_triangular)/triangular_solve | solution.py:65
  172.7 8.0 %fusion.85 = f32[512,4096]{1,0:T(8,128)} fusion(bf16[4096,512]{1,0:T(8,128)(2,1)} %all-gather.2.cloned.1.call-done, f32[128,512]{1,0:T(8,128)S(1)} %fusion.86, f32[128,512]{1,0:T(8,128)S(1)} %fusion.87, f32[128,512]{1,0:T(8,128)S(1)} %fusion.89, f32[128,512]{1,0:T(8,128)S(1)} %fusion.74), kind=kOutput, calls=%fused_computation.144 | convolution fusion | flops 2149318656 | bytes 13631488 | tf_op jit(solution)/shard_map/dot_general | solution.py:48
  180.7 5.7 %fusion.96 = f32[512,4096]{1,0:T(8,128)} fusion(bf16[4096,512]{1,0:T(8,128)(2,1)S(1)} %copy-done, f32[128,512]{1,0:T(8,128)S(1)} %fusion.86, f32[128,512]{1,0:T(8,128)S(1)} %fusion.87, f32[128,512]{1,0:T(8,128)S(1)} %fusion.89, f32[128,512]{1,0:T(8,128)S(1)} %fusion.74), kind=kOutput, calls=%fused_computation.167 | convolution fusion | flops 2149580800 | bytes 13631488 | tf_op jit(solution)/shard_map/dot_general | solution.py:48
  186.4 8.3 %add_convert_fusion = bf16[512,4096]{1,0:T(8,128)(2,1)S(1)} fusion(f32[512,4096]{1,0:T(8,128)} %fusion.85, f32[512,4096]{1,0:T(8,128)} %fusion.96, bf16[4096,512]{1,0:T(8,128)(2,1)S(1)} %copy-done, f32[128,512]{1,0:T(8,128)S(1)} %fusion.86, f32[128,512]{1,0:T(8,128)S(1)} %fusion.87, f32[128,512]{1,0:T(8,128)S(1)} %fusion.89, f32[128,512]{1,0:T(8,128)S(1)} %fusion.74), kind=kOutput, calls=%fused_computation.3 | convolution fusion | flops 2155085824 | bytes 26214400 | tf_op jit(solution)/shard_map/dot_general | solution.py:48
  194.8 4.5 %fusion = f32[256,512]{1,0:T(8,128)S(1)} fusion(bf16[512,4096]{1,0:T(8,128)(2,1)S(1)} %add_convert_fusion, bf16[2048,4096]{1,0:T(8,128)(2,1)} %param.6, s32[]{:T(128)S(6)} %select_n.284, bf16[4096]{0:T(1024)(128)(2,1)S(1)} %bitcast.208), kind=kOutput, calls=%fused_computation.4 | convolution fusion | flops 1077936128 | bytes 6823940 | tf_op jit(solution)/shard_map/dot_general | solution.py:78
  199.3 8.1 %collective-permute-start.7 = (f32[256,512]{1,0:T(8,128)S(1)}, f32[256,512]{1,0:T(8,128)S(1)}, u32[]{:S(2)}, u32[]{:S(2)}) collective-permute-start(f32[256,512]{1,0:T(8,128)S(1)} %fusion), channel_id=1, source_target_pairs={{0,7},{1,0},{2,1},{3,2},{4,3},{5,4},{6,5},{7,6},{8,15},{9,8},{10,9... | collective-permute-start | bytes 1572872 | tf_op jit(solution)/shard_map/ppermute | solution.py:13
  213.0 3.8 fusion.6
  216.8 3.8 fusion.9
  222.6 3.8 fusion.12
  227.1 3.9 fusion.15
  231.0 3.8 fusion.18
  239.5 25.6 %collective-permute-done.4 = f32[256,512]{1,0:T(8,128)} collective-permute-done((f32[256,512]{1,0:T(8,128)}, f32[256,512]{1,0:T(8,128)}, u32[]{:S(2)}, u32[]{:S(2)}) %collective-permute-start.4) | collective-permute-done | bytes 524320 | tf_op jit(solution)/shard_map/ppermute | solution.py:13
  267.8 4.0 %fusion.47 = f32[256,512]{1,0:T(8,128)S(1)} fusion(f32[256,512]{1,0:T(8,128)S(1)} %collective-permute-done.7, f32[256,512]{1,0:T(8,128)} %collective-permute-done.6, f32[256,512]{1,0:T(8,128)} %collective-permute-done.5, f32[256,512]{1,0:T(8,128)} %collective-permute-done.4, f32[256,512]{1,0:T(8,128)} %collective-permute-done.3, ...), kind=kOutput, calls=%fused_computation.44 | convolution fusion | flops 1078984704 | bytes 10493956 | tf_op jit(solution)/shard_map/dot_general | solution.py:78
  284.5 4.5 %collective-permute-done.9 = f32[64,512]{1,0:T(8,128)} collective-permute-done((f32[64,512]{1,0:T(8,128)S(1)}, f32[64,512]{1,0:T(8,128)}, u32[]{:S(2)}, u32[]{:S(2)}) %collective-permute-start.9) | collective-permute-done | bytes 131104 | tf_op jit(solution)/shard_map/ppermute | solution.py:13
  295.3 8.8 %collective-permute-start.28 = (f32[4,512]{1,0:T(4,128)S(1)}, f32[4,512]{1,0:T(4,128)S(1)}, u32[]{:S(2)}, u32[]{:S(2)}) collective-permute-start(f32[4,512]{1,0:T(4,128)S(1)} %get-tuple-element.33), channel_id=1, source_target_pairs={{0,112},{8,120},{16,0},{24,8},{32,16},{40,24},{48,32},{56,40},{64,... | collective-permute-start | bytes 24584 | tf_op jit(solution)/shard_map/ppermute | solution.py:13
  307.6 4.1 %collective-permute-start.25 = (f32[4,512]{1,0:T(4,128)S(1)}, f32[4,512]{1,0:T(4,128)S(1)}, u32[]{:S(2)}, u32[]{:S(2)}) collective-permute-start(f32[4,512]{1,0:T(4,128)S(1)} %get-tuple-element.36), channel_id=1, source_target_pairs={{0,88},{8,96},{16,104},{24,112},{32,120},{40,0},{48,8},{56,16},{64... | collective-permute-start | bytes 24584 | tf_op jit(solution)/shard_map/ppermute | solution.py:13
  311.6 4.4 %collective-permute-start.23 = (f32[4,512]{1,0:T(4,128)S(1)}, f32[4,512]{1,0:T(4,128)S(1)}, u32[]{:S(2)}, u32[]{:S(2)}) collective-permute-start(f32[4,512]{1,0:T(4,128)S(1)} %get-tuple-element.38), channel_id=1, source_target_pairs={{0,72},{8,80},{16,88},{24,96},{32,104},{40,112},{48,120},{56,0},{6... | collective-permute-start | bytes 24584 | tf_op jit(solution)/shard_map/ppermute | solution.py:13
  323.0 5.4 %collective-permute-start.17 = (f32[4,512]{1,0:T(4,128)S(1)}, f32[4,512]{1,0:T(4,128)S(1)}, u32[]{:S(2)}, u32[]{:S(2)}) collective-permute-start(f32[4,512]{1,0:T(4,128)S(1)} %get-tuple-element.44), channel_id=1, source_target_pairs={{0,24},{8,32},{16,40},{24,48},{32,56},{40,64},{48,72},{56,80},{64,... | collective-permute-start | bytes 24584 | tf_op jit(solution)/shard_map/ppermute | solution.py:13
  329.9 4.7 %collective-permute-done.16 = f32[4,512]{1,0:T(4,128)S(1)} collective-permute-done((f32[4,512]{1,0:T(4,128)S(1)}, f32[4,512]{1,0:T(4,128)S(1)}, u32[]{:S(2)}, u32[]{:S(2)}) %collective-permute-start.16) | collective-permute-done | bytes 8224 | tf_op jit(solution)/shard_map/ppermute | solution.py:13
  335.4 4.5 %gather_fusion = f32[512]{0:T(512)S(1)} fusion(f32[512,512]{1,0:T(8,128)S(1)} %get-tuple-element.21, s32[512]{0:T(512)S(1)} %bitcast.200), kind=kCustom, calls=%fused_computation | custom fusion | bytes 8192 | tf_op jit(solution)/shard_map/jit(diagonal)/cond/branch_0_fun/gather | solution.py:88
  353.8 4.0 %collective-permute-start.40 = (f32[4,512]{1,0:T(4,128)S(1)}, f32[4,512]{1,0:T(4,128)S(1)}, u32[]{:S(2)}, u32[]{:S(2)}) collective-permute-start(f32[4,512]{1,0:T(4,128)S(1)} %get-tuple-element.19), channel_id=1, source_target_pairs={{0,40},{8,48},{16,56},{24,64},{32,72},{40,80},{48,88},{56,96},{64,... | collective-permute-start | bytes 24584 | tf_op jit(solution)/shard_map/ppermute | solution.py:13
  (238 shorter events, 116.1 us)
Async XLA Ops:
  7.2 165.5 %all-gather.2.cloned.1.call-start = ((), (), s32[]{:S(2)}) async-start(), calls=%async_computation | async-start | bytes 4456448 | tf_op jit(solution)/shard_map/all_gather | solution.py:62
  7.2 13.3 %collective-permute-start = (bf16[256,512]{1,0:T(8,128)(2,1)}, bf16[256,512]{1,0:T(8,128)(2,1)S(1)}, u32[]{:S(2)}, u32[]{:S(2)}) collective-permute-start(bf16[256,512]{1,0:T(8,128)(2,1)} %param.4), channel_id=1, source_target_pairs={{0,0},{16,1},{32,2},{48,3},{64,4},{80,5},{96,6},{112,7},{1,8},{17,... | collective-permute-start | bytes 786440 | tf_op jit(solution)/shard_map/ppermute | solution.py:61
  199.3 35.5 %collective-permute-start.7 = (f32[256,512]{1,0:T(8,128)S(1)}, f32[256,512]{1,0:T(8,128)S(1)}, u32[]{:S(2)}, u32[]{:S(2)}) collective-permute-start(f32[256,512]{1,0:T(8,128)S(1)} %fusion), channel_id=1, source_target_pairs={{0,7},{1,0},{2,1},{3,2},{4,3},{5,4},{6,5},{7,6},{8,15},{9,8},{10,9... | collective-permute-start | bytes 1572872 | tf_op jit(solution)/shard_map/ppermute | solution.py:13
  210.4 25.5 %collective-permute-start.6 = (f32[256,512]{1,0:T(8,128)S(1)}, f32[256,512]{1,0:T(8,128)}, u32[]{:S(2)}, u32[]{:S(2)}) collective-permute-start(f32[256,512]{1,0:T(8,128)S(1)} %fusion.3), channel_id=1, source_target_pairs={{0,6},{1,7},{2,0},{3,1},{4,2},{5,3},{6,4},{7,5},{8,14},{9,15},{10,... | collective-permute-start | bytes 1572872 | tf_op jit(solution)/shard_map/ppermute | solution.py:13
  216.8 22.7 %collective-permute-start.5 = (f32[256,512]{1,0:T(8,128)}, f32[256,512]{1,0:T(8,128)}, u32[]{:S(2)}, u32[]{:S(2)}) collective-permute-start(f32[256,512]{1,0:T(8,128)} %fusion.6), channel_id=1, source_target_pairs={{0,5},{1,6},{2,7},{3,0},{4,1},{5,2},{6,3},{7,4},{8,13},{9,14},{10,... | collective-permute-start | bytes 1572872 | tf_op jit(solution)/shard_map/ppermute | solution.py:13
  220.6 44.5 %collective-permute-start.4 = (f32[256,512]{1,0:T(8,128)}, f32[256,512]{1,0:T(8,128)}, u32[]{:S(2)}, u32[]{:S(2)}) collective-permute-start(f32[256,512]{1,0:T(8,128)} %fusion.9), channel_id=1, source_target_pairs={{0,4},{1,5},{2,6},{3,7},{4,0},{5,1},{6,2},{7,3},{8,12},{9,13},{10,... | collective-permute-start | bytes 1572872 | tf_op jit(solution)/shard_map/ppermute | solution.py:13
  226.4 38.6 %collective-permute-start.3 = (f32[256,512]{1,0:T(8,128)}, f32[256,512]{1,0:T(8,128)}, u32[]{:S(2)}, u32[]{:S(2)}) collective-permute-start(f32[256,512]{1,0:T(8,128)} %fusion.12), channel_id=1, source_target_pairs={{0,3},{1,4},{2,5},{3,6},{4,7},{5,0},{6,1},{7,2},{8,11},{9,12},{10,... | collective-permute-start | bytes 1572872 | tf_op jit(solution)/shard_map/ppermute | solution.py:13
  234.8 30.2 %collective-permute-start.2 = (f32[256,512]{1,0:T(8,128)}, f32[256,512]{1,0:T(8,128)}, u32[]{:S(2)}, u32[]{:S(2)}) collective-permute-start(f32[256,512]{1,0:T(8,128)} %fusion.15), channel_id=1, source_target_pairs={{0,2},{1,3},{2,4},{3,5},{4,6},{5,7},{6,0},{7,1},{8,10},{9,11},{10,... | collective-permute-start | bytes 1572872 | tf_op jit(solution)/shard_map/ppermute | solution.py:13
  235.9 31.8 %collective-permute-start.1 = (f32[256,512]{1,0:T(8,128)}, f32[256,512]{1,0:T(8,128)}, u32[]{:S(2)}, u32[]{:S(2)}) collective-permute-start(f32[256,512]{1,0:T(8,128)} %fusion.18), channel_id=1, source_target_pairs={{0,1},{1,2},{2,3},{3,4},{4,5},{5,6},{6,7},{7,0},{8,9},{9,10},{10,1... | collective-permute-start | bytes 1572872 | tf_op jit(solution)/shard_map/ppermute | solution.py:13
  280.0 9.0 %collective-permute-start.9 = (f32[64,512]{1,0:T(8,128)S(1)}, f32[64,512]{1,0:T(8,128)}, u32[]{:S(2)}, u32[]{:S(2)}) collective-permute-start(f32[64,512]{1,0:T(8,128)S(1)} %get-tuple-element.30), channel_id=1, source_target_pairs={{0,2},{1,3},{2,4},{3,5},{4,6},{5,7},{6,0},{7,1},{8,10},{9,11},{10,... | collective-permute-start | bytes 393224 | tf_op jit(solution)/shard_map/ppermute | solution.py:13
  281.9 8.6 %collective-permute-start.8 = (f32[64,512]{1,0:T(8,128)S(1)}, f32[64,512]{1,0:T(8,128)}, u32[]{:S(2)}, u32[]{:S(2)}) collective-permute-start(f32[64,512]{1,0:T(8,128)S(1)} %get-tuple-element.24), channel_id=1, source_target_pairs={{0,1},{1,2},{2,3},{3,4},{4,5},{5,6},{6,7},{7,0},{8,9},{9,10},{10,1... | collective-permute-start | bytes 393224 | tf_op jit(solution)/shard_map/ppermute | solution.py:13
  291.9 19.8 %collective-permute-start.29 = (f32[4,512]{1,0:T(4,128)S(1)}, f32[4,512]{1,0:T(4,128)S(1)}, u32[]{:S(2)}, u32[]{:S(2)}) collective-permute-start(f32[4,512]{1,0:T(4,128)S(1)} %get-tuple-element.32), channel_id=1, source_target_pairs={{0,120},{8,0},{16,8},{24,16},{32,24},{40,32},{48,40},{56,48},{64,5... | collective-permute-start | bytes 24584 | tf_op jit(solution)/shard_map/ppermute | solution.py:13
  295.3 16.4 %collective-permute-start.28 = (f32[4,512]{1,0:T(4,128)S(1)}, f32[4,512]{1,0:T(4,128)S(1)}, u32[]{:S(2)}, u32[]{:S(2)}) collective-permute-start(f32[4,512]{1,0:T(4,128)S(1)} %get-tuple-element.33), channel_id=1, source_target_pairs={{0,112},{8,120},{16,0},{24,8},{32,16},{40,24},{48,32},{56,40},{64,... | collective-permute-start | bytes 24584 | tf_op jit(solution)/shard_map/ppermute | solution.py:13
  304.1 12.0 %collective-permute-start.27 = (f32[4,512]{1,0:T(4,128)S(1)}, f32[4,512]{1,0:T(4,128)S(1)}, u32[]{:S(2)}, u32[]{:S(2)}) collective-permute-start(f32[4,512]{1,0:T(4,128)S(1)} %get-tuple-element.34), channel_id=1, source_target_pairs={{0,104},{8,112},{16,120},{24,0},{32,8},{40,16},{48,24},{56,32},{64... | collective-permute-start | bytes 24584 | tf_op jit(solution)/shard_map/ppermute | solution.py:13
  304.1 12.0 %collective-permute-start.26 = (f32[4,512]{1,0:T(4,128)S(1)}, f32[4,512]{1,0:T(4,128)S(1)}, u32[]{:S(2)}, u32[]{:S(2)}) collective-permute-start(f32[4,512]{1,0:T(4,128)S(1)} %get-tuple-element.35), channel_id=1, source_target_pairs={{0,96},{8,104},{16,112},{24,120},{32,0},{40,8},{48,16},{56,24},{64... | collective-permute-start | bytes 24584 | tf_op jit(solution)/shard_map/ppermute | solution.py:13
  307.6 10.9 %collective-permute-start.25 = (f32[4,512]{1,0:T(4,128)S(1)}, f32[4,512]{1,0:T(4,128)S(1)}, u32[]{:S(2)}, u32[]{:S(2)}) collective-permute-start(f32[4,512]{1,0:T(4,128)S(1)} %get-tuple-element.36), channel_id=1, source_target_pairs={{0,88},{8,96},{16,104},{24,112},{32,120},{40,0},{48,8},{56,16},{64... | collective-permute-start | bytes 24584 | tf_op jit(solution)/shard_map/ppermute | solution.py:13
  311.6 10.5 %collective-permute-start.23 = (f32[4,512]{1,0:T(4,128)S(1)}, f32[4,512]{1,0:T(4,128)S(1)}, u32[]{:S(2)}, u32[]{:S(2)}) collective-permute-start(f32[4,512]{1,0:T(4,128)S(1)} %get-tuple-element.38), channel_id=1, source_target_pairs={{0,72},{8,80},{16,88},{24,96},{32,104},{40,112},{48,120},{56,0},{6... | collective-permute-start | bytes 24584 | tf_op jit(solution)/shard_map/ppermute | solution.py:13
  316.1 12.4 %collective-permute-start.21 = (f32[4,512]{1,0:T(4,128)S(1)}, f32[4,512]{1,0:T(4,128)S(1)}, u32[]{:S(2)}, u32[]{:S(2)}) collective-permute-start(f32[4,512]{1,0:T(4,128)S(1)} %get-tuple-element.40), channel_id=1, source_target_pairs={{0,56},{8,64},{16,72},{24,80},{32,88},{40,96},{48,104},{56,112},{6... | collective-permute-start | bytes 24584 | tf_op jit(solution)/shard_map/ppermute | solution.py:13
  318.5 10.0 %collective-permute-start.20 = (f32[4,512]{1,0:T(4,128)S(1)}, f32[4,512]{1,0:T(4,128)S(1)}, u32[]{:S(2)}, u32[]{:S(2)}) collective-permute-start(f32[4,512]{1,0:T(4,128)S(1)} %get-tuple-element.41), channel_id=1, source_target_pairs={{0,48},{8,56},{16,64},{24,72},{32,80},{40,88},{48,96},{56,104},{64... | collective-permute-start | bytes 24584 | tf_op jit(solution)/shard_map/ppermute | solution.py:13
  318.5 10.1 %collective-permute-start.19 = (f32[4,512]{1,0:T(4,128)S(1)}, f32[4,512]{1,0:T(4,128)S(1)}, u32[]{:S(2)}, u32[]{:S(2)}) collective-permute-start(f32[4,512]{1,0:T(4,128)S(1)} %get-tuple-element.42), channel_id=1, source_target_pairs={{0,40},{8,48},{16,56},{24,64},{32,72},{40,80},{48,88},{56,96},{64,... | collective-permute-start | bytes 24584 | tf_op jit(solution)/shard_map/ppermute | solution.py:13
  334.6 11.0 %collective-permute-start.30 = (f32[4,512]{1,0:T(4,128)S(1)}, f32[4,512]{1,0:T(4,128)S(1)}, u32[]{:S(2)}, u32[]{:S(2)}) collective-permute-start(f32[4,512]{1,0:T(4,128)S(1)} %get-tuple-element.19), channel_id=1, source_target_pairs={{0,120},{8,0},{16,8},{24,16},{32,24},{40,32},{48,40},{56,48},{64,5... | collective-permute-start | bytes 24584 | tf_op jit(solution)/shard_map/ppermute | solution.py:13
  340.1 10.4 %collective-permute-start.33 = (f32[4,512]{1,0:T(4,128)S(1)}, f32[4,512]{1,0:T(4,128)S(1)}, u32[]{:S(2)}, u32[]{:S(2)}) collective-permute-start(f32[4,512]{1,0:T(4,128)S(1)} %get-tuple-element.19), channel_id=1, source_target_pairs={{0,96},{8,104},{16,112},{24,120},{32,0},{40,8},{48,16},{56,24},{64... | collective-permute-start | bytes 24584 | tf_op jit(solution)/shard_map/ppermute | solution.py:13
  343.0 8.1 %collective-permute-start.34 = (f32[4,512]{1,0:T(4,128)S(1)}, f32[4,512]{1,0:T(4,128)S(1)}, u32[]{:S(2)}, u32[]{:S(2)}) collective-permute-start(f32[4,512]{1,0:T(4,128)S(1)} %get-tuple-element.19), channel_id=1, source_target_pairs={{0,88},{8,96},{16,104},{24,112},{32,120},{40,0},{48,8},{56,16},{64... | collective-permute-start | bytes 24584 | tf_op jit(solution)/shard_map/ppermute | solution.py:13
  345.6 8.2 %collective-permute-start.35 = (f32[4,512]{1,0:T(4,128)S(1)}, f32[4,512]{1,0:T(4,128)S(1)}, u32[]{:S(2)}, u32[]{:S(2)}) collective-permute-start(f32[4,512]{1,0:T(4,128)S(1)} %get-tuple-element.19), channel_id=1, source_target_pairs={{0,80},{8,88},{16,96},{24,104},{32,112},{40,120},{48,0},{56,8},{64... | collective-permute-start | bytes 24584 | tf_op jit(solution)/shard_map/ppermute | solution.py:13
  347.4 10.4 %collective-permute-start.36 = (f32[4,512]{1,0:T(4,128)S(1)}, f32[4,512]{1,0:T(4,128)S(1)}, u32[]{:S(2)}, u32[]{:S(2)}) collective-permute-start(f32[4,512]{1,0:T(4,128)S(1)} %get-tuple-element.19), channel_id=1, source_target_pairs={{0,72},{8,80},{16,88},{24,96},{32,104},{40,112},{48,120},{56,0},{6... | collective-permute-start | bytes 24584 | tf_op jit(solution)/shard_map/ppermute | solution.py:13
  347.6 10.3 %collective-permute-start.37 = (f32[4,512]{1,0:T(4,128)S(1)}, f32[4,512]{1,0:T(4,128)S(1)}, u32[]{:S(2)}, u32[]{:S(2)}) collective-permute-start(f32[4,512]{1,0:T(4,128)S(1)} %get-tuple-element.19), channel_id=1, source_target_pairs={{0,64},{8,72},{16,80},{24,88},{32,96},{40,104},{48,112},{56,120},{... | collective-permute-start | bytes 24584 | tf_op jit(solution)/shard_map/ppermute | solution.py:13
  350.5 10.4 %collective-permute-start.38 = (f32[4,512]{1,0:T(4,128)S(1)}, f32[4,512]{1,0:T(4,128)S(1)}, u32[]{:S(2)}, u32[]{:S(2)}) collective-permute-start(f32[4,512]{1,0:T(4,128)S(1)} %get-tuple-element.19), channel_id=1, source_target_pairs={{0,56},{8,64},{16,72},{24,80},{32,88},{40,96},{48,104},{56,112},{6... | collective-permute-start | bytes 24584 | tf_op jit(solution)/shard_map/ppermute | solution.py:13
  351.1 10.2 %collective-permute-start.39 = (f32[4,512]{1,0:T(4,128)S(1)}, f32[4,512]{1,0:T(4,128)S(1)}, u32[]{:S(2)}, u32[]{:S(2)}) collective-permute-start(f32[4,512]{1,0:T(4,128)S(1)} %get-tuple-element.19), channel_id=1, source_target_pairs={{0,48},{8,56},{16,64},{24,72},{32,80},{40,88},{48,96},{56,104},{64... | collective-permute-start | bytes 24584 | tf_op jit(solution)/shard_map/ppermute | solution.py:13
  353.8 8.7 %collective-permute-start.40 = (f32[4,512]{1,0:T(4,128)S(1)}, f32[4,512]{1,0:T(4,128)S(1)}, u32[]{:S(2)}, u32[]{:S(2)}) collective-permute-start(f32[4,512]{1,0:T(4,128)S(1)} %get-tuple-element.19), channel_id=1, source_target_pairs={{0,40},{8,48},{16,56},{24,64},{32,72},{40,80},{48,88},{56,96},{64,... | collective-permute-start | bytes 24584 | tf_op jit(solution)/shard_map/ppermute | solution.py:13
  367.3 8.1 %collective-permute-start.45 = (f32[64,512]{1,0:T(8,128)S(1)}, f32[64,512]{1,0:T(8,128)S(1)}, u32[]{:S(2)}, u32[]{:S(2)}) collective-permute-start(f32[64,512]{1,0:T(8,128)S(1)} %reshape.124), channel_id=1, source_target_pairs={{0,7},{1,0},{2,1},{3,2},{4,3},{5,4},{6,5},{7,6},{8,15},{9,8},{10,9... | collective-permute-start | bytes 393224 | tf_op jit(solution)/shard_map/ppermute | solution.py:13
  372.0 9.2 %collective-permute-start.49 = (f32[64,512]{1,0:T(8,128)S(1)}, f32[64,512]{1,0:T(8,128)S(1)}, u32[]{:S(2)}, u32[]{:S(2)}) collective-permute-start(f32[64,512]{1,0:T(8,128)S(1)} %reshape.124), channel_id=1, source_target_pairs={{0,3},{1,4},{2,5},{3,6},{4,7},{5,0},{6,1},{7,2},{8,11},{9,12},{10,... | collective-permute-start | bytes 393224 | tf_op jit(solution)/shard_map/ppermute | solution.py:13
  375.7 8.1 %collective-permute-start.51 = (f32[64,512]{1,0:T(8,128)S(1)}, f32[64,512]{1,0:T(8,128)S(1)}, u32[]{:S(2)}, u32[]{:S(2)}) collective-permute-start(f32[64,512]{1,0:T(8,128)S(1)} %reshape.124), channel_id=1, source_target_pairs={{0,1},{1,2},{2,3},{3,4},{4,5},{5,6},{6,7},{7,0},{8,9},{9,10},{10,1... | collective-permute-start | bytes 393224 | tf_op jit(solution)/shard_map/ppermute | solution.py:13
  (29 other events, 443.7 us)
Sparse Core Ops, SparseCore 0:
  21.4 65.2 all-gather.1
